TPU v7x, 128 devices: a whole 4x4x4 slice. The times are simulated.
128 devices in a mesh: mode: 8 (over x, core), member: 16 (over z, y).
Axes of the slice: x: 4, y: 4, z: 4, core: 2. Of those that a mesh axis runs over, the one named last changes fastest.
Arguments:
- ground_accel: bfloat16 [4, 639], replicated, may hold values from -6 to 6
- modal_kernel: bfloat16 [4096, 512], P(('mode', 'member')), may hold values from -0.25 to 0.25
- mode_shapes: bfloat16 [98304, 4096], P('member', 'mode'), may hold values from -0.09375 to 0.09375
- member_owner: int32 [16384, 1], P('member'), may hold values from 0 to 127; in each aligned block of 128 rows (0 to 127, 128 to 255, ...) at most 2 rows name the same one
- member_group: int32 [16384, 1], P('member'), may hold values from 0 to 3
- record_table: int32 [512, 8], P(('mode', 'member')), may hold values from 0 to 3
- case_coef: float32 [8, 6], replicated, may hold values from -1.5 to 1.5
- gravity: float32 [512, 8], P(('mode', 'member')), may hold values from -10 to 10
Outputs:
- demand: float32 [512, 8], P(('mode', 'member'))
Inputs may be any that keep to these rules, and one draw needn't show every extreme that they name: `member_owner`: in each aligned block of 1024 / 8 members no owner is named more than 2 times, a bound that some block reaches.
All inputs are finite; a program needn't handle non-finite values.
Results may differ from a plain program's by a relative error of at most 0.0065.
Values may be sent and summed in bfloat16 or wider, within the bound.
No kernel may reach another device: no remote copies, remote signals or barrier semaphores. Data moves between devices by JAX's collectives and lax.ppermute only.
A program may use at most 64 MiB of HBM per device.

v0:
```python
import jax
import jax.numpy as jnp
from jax import lax
from jax.sharding import PartitionSpec as P


def lagged_table(ground_accel, tap_count):
    record_count, span_len = ground_accel.shape
    step_count = span_len - tap_count + 1
    tiled = jnp.tile(ground_accel, (1, step_count + 1))[:, : step_count * (span_len + 1)]
    windows = tiled.reshape(record_count, step_count, span_len + 1)[:, :, :tap_count]
    return windows.reshape(record_count * step_count, tap_count)


def local(
    ground_accel,
    modal_kernel,
    mode_shapes,
    member_owner,
    member_group,
    record_table,
    case_coef,
    gravity,
):
    tap_count = modal_kernel.shape[1]
    record_count = ground_accel.shape[0]
    comp_count = case_coef.shape[1]
    n_mode = lax.axis_size("mode")
    n_member = lax.axis_size("member")
    groups_here = gravity.shape[0]
    group_total = groups_here * n_mode * n_member
    lagged = lagged_table(ground_accel, tap_count)
    local_resp = lax.dot_general(
        modal_kernel[:, ::-1], lagged, (((1,), (1,)), ((), ())), preferred_element_type=jnp.float32
    ).astype(jnp.bfloat16)
    modal_resp = lax.all_gather(local_resp, "member", axis=0, tiled=True)
    partial = jnp.dot(mode_shapes, modal_resp, preferred_element_type=jnp.float32).astype(
        jnp.bfloat16
    )
    members_here = member_owner.shape[0]
    packed = partial.reshape(members_here, comp_count * partial.shape[1])
    group_index = member_owner[:, 0] * groups_here + member_group[:, 0]
    selector = (jnp.arange(group_total)[:, None] == group_index[None, :]).astype(jnp.bfloat16)
    group_part = jnp.dot(selector, packed, preferred_element_type=jnp.float32)
    by_mode = lax.psum_scatter(
        group_part.astype(jnp.bfloat16), "mode", scatter_dimension=0, tiled=True
    )
    group_sums = lax.psum_scatter(
        by_mode.astype(jnp.float32), "member", scatter_dimension=0, tiled=True
    )
    group_sums = group_sums.reshape(groups_here, comp_count, record_count, -1)
    case_mix = jnp.einsum("sc,gcrt->gsrt", case_coef, group_sums, precision=lax.Precision.HIGHEST)
    record_pick = (record_table[:, :, None] == jnp.arange(record_count)[None, None, :]).astype(
        jnp.float32
    )
    selected = jnp.sum(record_pick[:, :, :, None] * case_mix, axis=2)
    combined = gravity[:, :, None] + selected
    return jnp.max(jnp.abs(combined), axis=2)


def solution(mesh):
    placed = (
        P(),
        P(("mode", "member"), None),
        P("member", "mode"),
        P("member", None),
        P("member", None),
        P(("mode", "member"), None),
        P(),
        P(("mode", "member"), None),
    )
    return jax.shard_map(
        local, mesh=mesh, in_specs=placed, out_specs=P(("mode", "member"), None), check_vma=False
    )
```

profile of v0, /device:TPU:0, one launch (start us, length us, event | category | flops | bytes accessed | tf_op | source)
XLA Modules:
  0.0 198.6 jit_solution(844657869856164750)
XLA Ops:
  6.5 0.0 copy-start
  6.5 0.0 reduce-scatter.2.cloned.1.call-start
  6.5 0.8 tile.4
  7.3 0.6 tile.10
  7.9 0.2 slice.8
  8.2 0.1 copy.21
  8.3 1.6 rev.3
  9.9 0.2 convolution_convert_fusion.2
  10.2 25.6 %all_gather.3 = bf16[512,512]{1,0:T(8,128)(2,1)S(1)} all-gather(bf16[32,512]{1,0:T(8,128)(2,1)S(1)} %convolution_convert_fusion.2), channel_id=1, replica_groups=mesh['mode'=8,'member'=16] {'member'}, dimensions={0}, use_global_device_ids=true | all-gather | bytes 557056 | tf_op jit(solution)/shard_map/all_gather | solution.py:36
  35.8 8.2 %fusion = bf16[6144,512]{0,1:T(8,128)(2,1)} fusion(bf16[512,512]{1,0:T(8,128)(2,1)S(1)} %all_gather.3, bf16[6144,512]{1,0:T(8,128)(2,1)} %param.10), kind=kOutput, calls=%fused_computation.1 | convolution fusion | flops 3224371200 | bytes 13107200 | tf_op jit(solution)/shard_map/dot_general | solution.py:37
  44.0 8.7 %copy.14 = bf16[6144,512]{1,0:T(8,128)(2,1)} copy(bf16[6144,512]{0,1:T(8,128)(2,1)} %fusion) | data formatting | bytes 12582912 | tf_op jit(solution)/shard_map/convert_element_type | solution.py:37
  52.7 11.5 %reshape.37 = bf16[1024,3072]{1,0:T(8,128)(2,1)} reshape(bf16[6144,512]{1,0:T(8,128)(2,1)} %copy.14) | data formatting | bytes 12582912 | tf_op jit(solution)/shard_map/reshape | solution.py:41
  64.2 0.0 copy-done.2
  64.2 0.0 copy-start.5
  64.2 0.0 copy-start.3
  64.2 0.0 copy-start.4
  64.3 7.6 %convolution_convert_fusion.1 = bf16[512,3072]{1,0:T(8,128)(2,1)} fusion(bf16[1024,3072]{1,0:T(8,128)(2,1)} %reshape.37, s32[1024]{0:T(1024)S(1)} %bitcast.28), kind=kOutput, calls=%fused_computation.2 | convolution fusion | flops 3223322624 | bytes 9441280 | tf_op jit(solution)/shard_map/dot_general | solution.py:44
  71.8 0.0 reduce-scatter.2.cloned.1.call-update
  71.8 0.0 copy-done.5
  71.9 0.6 dynamic-slice
  73.1 33.8 %reduce-scatter.2.cloned.1.call-done = bf16[64,3072]{1,0:T(8,128)(2,1)} async-done(((bf16[512,3072]{1,0:T(8,128)(2,1)}), bf16[64,3072]{1,0:T(8,128)(2,1)}) %reduce-scatter.2.cloned.1.call-update) | async-done | bytes 393232 | tf_op jit(solution)/shard_map/reduce_scatter | solution.py:45
  107.0 83.7 %all-reduce.2 = f32[64,3072]{1,0:T(8,128)S(1)} all-reduce(bf16[64,3072]{1,0:T(8,128)(2,1)} %reduce-scatter.2.cloned.1.call-done), channel_id=3, replica_groups=mesh['mode'=8,'member'=16] {'member'}, use_global_device_ids=true, to_apply=%region_1.0.clone | all-reduce | flops 196608 | bytes 1179648
  190.8 0.2 fusion.2
  191.0 0.7 abs_reduce_fusion
  (11 shorter events, 0.1 us)
Async XLA Ops:
  6.5 184.2 %copy-start = (f32[8,6]{1,0:T(8,128)S(1)}, f32[8,6]{1,0:T(8,128)}, u32[]{:S(2)}) copy-start(f32[8,6]{1,0:T(8,128)} %param.14) | copy-start | bytes 580
  6.5 100.4 %reduce-scatter.2.cloned.1.call-start = ((), (), s32[]{:S(2)}) async-start(), calls=%async_computation.1 | async-start | bytes 3538944 | tf_op jit(solution)/shard_map/reduce_scatter | solution.py:45
  52.7 11.5 %copy-start.1 = (s32[1024,1]{0,1:T(1,128)S(1)}, s32[1024,1]{0,1:T(1,128)}, u32[]{:S(2)}) copy-start(s32[1024,1]{0,1:T(1,128)} %param.12) | copy-start | bytes 12292
  52.7 11.5 %copy-start.2 = (s32[1024,1]{0,1:T(1,128)S(1)}, s32[1024,1]{0,1:T(1,128)}, u32[]{:S(2)}) copy-start(s32[1024,1]{0,1:T(1,128)} %param.11) | copy-start | bytes 12292
  64.2 7.6 %copy-start.5 = (u32[128]{0:T(128)S(1)}, u32[128]{0:T(128)}, u32[]{:S(2)}) copy-start(u32[128]{0:T(128)} %constant.11) | copy-start | bytes 1540
  64.2 8.9 %copy-start.3 = (s32[4,8]{1,0:T(4,128)S(1)}, s32[4,8]{1,0:T(4,128)}, u32[]{:S(2)}) copy-start(s32[4,8]{1,0:T(4,128)} %param.13) | copy-start | bytes 388
  64.2 126.7 %copy-start.4 = (f32[4,8]{1,0:T(4,128)S(1)}, f32[4,8]{1,0:T(4,128)}, u32[]{:S(2)}) copy-start(f32[4,8]{1,0:T(4,128)} %param.15) | copy-start | bytes 388
Sparse Core Ops, SparseCore 0:
  72.0 34.9 reduce-scatter.1
where the time goes:
time: 199 us
  blocking collectives  109 us (55%)
  waiting for transfers between devices  33.9 us (17%)
  local copies, waits for them, and re-layouts  24.2 us (12%)
  matrix products  16.2 us (8%)
  between operations  14.2 us (7%)
    unnamed x1, blocking collectives  83.7 us
    reduce_scatter x1, waiting for transfers between devices, local(): lax.psum_scatter(group_part.astype(jnp.bfloat16), 'mode', scatter_dimensi...  33.8 us
    all_gather x1, blocking collectives, local(): modal_resp = lax.all_gather(local_resp, 'member', axis=0, tiled=True)  25.6 us
    reshape x1, local copies, waits for them, and re-layouts, local(): packed = partial.reshape(members_here, comp_count * partial.shape[1])  11.5 us
    convert_element_type x1, local copies, waits for them, and re-layouts, local(): jnp.dot(mode_shapes, modal_resp, preferred_element_type=jnp.float32)  8.68 us
    dot_general x1, matrix products, local(): jnp.dot(mode_shapes, modal_resp, preferred_element_type=jnp.float32)  8.21 us
    dot_general x1, matrix products, local(): group_part = jnp.dot(selector, packed, preferred_element_type=jnp.float32)  7.56 us
  transfers between devices with their start and end apart: 1, of which 1 were waited for; matrix products, arithmetic and copies ran while one was open for 0% of the time, Pallas kernels for 0%

commit v1 on v0

--- a/solution.py
+++ b/solution.py
@@ -33,7 +33,9 @@
     local_resp = lax.dot_general(
         modal_kernel[:, ::-1], lagged, (((1,), (1,)), ((), ())), preferred_element_type=jnp.float32
     ).astype(jnp.bfloat16)
-    modal_resp = lax.all_gather(local_resp, "member", axis=0, tiled=True)
+    modal_resp = jnp.concatenate(
+        lax.all_to_all(jnp.stack([local_resp] * lax.axis_size("member")), "member", 0, 0), axis=0
+    )
     partial = jnp.dot(mode_shapes, modal_resp, preferred_element_type=jnp.float32).astype(
         jnp.bfloat16
     )

time: 199 us -> 192 us (0.965)
  blocking collectives: 109 us -> 83.7 us
  waiting for transfers between devices: 33.9 us -> 43.5 us
  starting transfers between devices: 0.01 us -> 8.17 us
    all_gather x1 -> x0, blocking collectives: 25.6 us -> none  [local(): modal_resp = lax.all_gather(local_resp, 'member', axis=0, tiled=True)]
    all_to_all x0 -> x1, waiting for transfers between devices: none -> 11.4 us  [local(): lax.all_to_all(jnp.stack([local_resp] * lax.axis_size('member')), 'member...]
    all_to_all x0 -> x1, starting transfers between devices: none -> 8.13 us  [local(): lax.all_to_all(jnp.stack([local_resp] * lax.axis_size('member')), 'member...]
  transfers between devices with their start and end apart: 1 -> 2, of which waited for: 1 -> 2; matrix products, arithmetic and copies ran while one was open for 0% -> 0% of each run, Pallas kernels for 0% -> 0%
where the time goes in v1:
time: 192 us
  blocking collectives  83.7 us (44%)
  waiting for transfers between devices  43.5 us (23%)
  local copies, waits for them, and re-layouts  25.1 us (13%)
  matrix products  16.2 us (8%)
  between operations  14.2 us (7%)
  starting transfers between devices  8.17 us (4%)
    unnamed x1, blocking collectives  83.7 us
    reduce_scatter x1, waiting for transfers between devices, local(): lax.psum_scatter(group_part.astype(jnp.bfloat16), 'mode', scatter_dimensi...  32 us
    reshape x1, local copies, waits for them, and re-layouts, local(): packed = partial.reshape(members_here, comp_count * partial.shape[1])  11.5 us
    all_to_all x1, waiting for transfers between devices, local(): lax.all_to_all(jnp.stack([local_resp] * lax.axis_size('member')), 'member...  11.4 us
    convert_element_type x1, local copies, waits for them, and re-layouts, local(): jnp.dot(mode_shapes, modal_resp, preferred_element_type=jnp.float32)  8.68 us
    dot_general x1, matrix products, local(): jnp.dot(mode_shapes, modal_resp, preferred_element_type=jnp.float32)  8.19 us
    all_to_all x1, starting transfers between devices, local(): lax.all_to_all(jnp.stack([local_resp] * lax.axis_size('member')), 'member...  8.13 us
    dot_general x1, matrix products, local(): group_part = jnp.dot(selector, packed, preferred_element_type=jnp.float32)  7.56 us
  transfers between devices with their start and end apart: 2, of which 2 were waited for; matrix products, arithmetic and copies ran while one was open for 0% of the time, Pallas kernels for 0%

profile of v1, /device:TPU:0, one launch (start us, length us, event | category | flops | bytes accessed | tf_op | source)
XLA Modules:
  0.0 191.6 jit_solution(14188243174455018353)
XLA Ops:
  6.5 0.0 copy-start
  6.5 0.8 tile.4
  7.3 0.6 tile.10
  8.0 0.2 slice.8
  8.2 0.1 copy.21
  8.3 1.6 rev.3
  10.0 0.2 convolution_convert_fusion.2
  10.2 0.9 stack.2
  11.1 8.1 %all-to-all-start = ((bf16[16,32,512]{2,1,0:T(8,128)(2,1)}), bf16[16,32,512]{2,1,0:T(8,128)(2,1)S(1)}, u32[]{:S(2)}, u32[]{:S(2)}) async-start(bf16[16,32,512]{2,1,0:T(8,128)(2,1)} %stack.2), calls=%async_computation | async-start | bytes 1048576 | tf_op jit(solution)/shard_map/all_to_all | solution.py:37
  19.2 0.0 reduce-scatter.2.cloned.1.call-start
  19.3 0.0 copy-done.2
  19.3 0.0 copy-done.1
  19.3 11.4 %all-to-all-done = bf16[16,32,512]{2,1,0:T(8,128)(2,1)S(1)} async-done(((bf16[16,32,512]{2,1,0:T(8,128)(2,1)}), bf16[16,32,512]{2,1,0:T(8,128)(2,1)S(1)}, u32[]{:S(2)}, u32[]{:S(2)}) %all-to-all-start) | async-done | bytes 524320 | tf_op jit(solution)/shard_map/all_to_all | solution.py:37
  30.8 8.2 %fusion = bf16[6144,512]{0,1:T(8,128)(2,1)} fusion(bf16[512,512]{1,0:T(8,128)(2,1)S(1)} %bitcast.29, bf16[6144,512]{1,0:T(8,128)(2,1)} %param.10), kind=kOutput, calls=%fused_computation.1 | convolution fusion | flops 3224371200 | bytes 13107200 | tf_op jit(solution)/shard_map/dot_general | solution.py:39
  39.0 8.7 %copy.14 = bf16[6144,512]{1,0:T(8,128)(2,1)} copy(bf16[6144,512]{0,1:T(8,128)(2,1)} %fusion) | data formatting | bytes 12582912 | tf_op jit(solution)/shard_map/convert_element_type | solution.py:39
  47.6 11.5 %reshape.43 = bf16[1024,3072]{1,0:T(8,128)(2,1)} reshape(bf16[6144,512]{1,0:T(8,128)(2,1)} %copy.14) | data formatting | bytes 12582912 | tf_op jit(solution)/shard_map/reshape | solution.py:43
  59.1 7.6 %convolution_convert_fusion.1 = bf16[512,3072]{1,0:T(8,128)(2,1)} fusion(bf16[1024,3072]{1,0:T(8,128)(2,1)} %reshape.43, s32[1024]{0:T(1024)S(1)} %bitcast.30), kind=kOutput, calls=%fused_computation.2 | convolution fusion | flops 3223322624 | bytes 9441280 | tf_op jit(solution)/shard_map/dot_general | solution.py:46
  66.7 0.0 reduce-scatter.2.cloned.1.call-update
  66.7 0.0 copy-done.5
  66.7 0.6 dynamic-slice
  68.0 32.0 %reduce-scatter.2.cloned.1.call-done = bf16[64,3072]{1,0:T(8,128)(2,1)} async-done(((bf16[512,3072]{1,0:T(8,128)(2,1)}), bf16[64,3072]{1,0:T(8,128)(2,1)}) %reduce-scatter.2.cloned.1.call-update) | async-done | bytes 393232 | tf_op jit(solution)/shard_map/reduce_scatter | solution.py:47
  100.0 83.7 %all-reduce.2 = f32[64,3072]{1,0:T(8,128)S(1)} all-reduce(bf16[64,3072]{1,0:T(8,128)(2,1)} %reduce-scatter.2.cloned.1.call-done), channel_id=3, replica_groups=mesh['mode'=8,'member'=16] {'member'}, use_global_device_ids=true, to_apply=%region_1.0.clone | all-reduce | flops 196608 | bytes 1179648
  183.8 0.2 fusion.2
  184.0 0.7 abs_reduce_fusion
  (13 shorter events, 0.1 us)
Async XLA Ops:
  6.5 177.2 %copy-start = (f32[8,6]{1,0:T(8,128)S(1)}, f32[8,6]{1,0:T(8,128)}, u32[]{:S(2)}) copy-start(f32[8,6]{1,0:T(8,128)} %param.14) | copy-start | bytes 580
  6.5 12.7 %copy-start.2 = (s32[1024,1]{0,1:T(1,128)S(1)}, s32[1024,1]{0,1:T(1,128)}, u32[]{:S(2)}) copy-start(s32[1024,1]{0,1:T(1,128)} %param.11) | copy-start | bytes 12292
  6.5 12.8 %copy-start.1 = (s32[1024,1]{0,1:T(1,128)S(1)}, s32[1024,1]{0,1:T(1,128)}, u32[]{:S(2)}) copy-start(s32[1024,1]{0,1:T(1,128)} %param.12) | copy-start | bytes 12292
  11.1 19.7 %all-to-all-start = ((bf16[16,32,512]{2,1,0:T(8,128)(2,1)}), bf16[16,32,512]{2,1,0:T(8,128)(2,1)S(1)}, u32[]{:S(2)}, u32[]{:S(2)}) async-start(bf16[16,32,512]{2,1,0:T(8,128)(2,1)} %stack.2), calls=%async_computation | async-start | bytes 1048576 | tf_op jit(solution)/shard_map/all_to_all | solution.py:37
  19.2 80.8 %reduce-scatter.2.cloned.1.call-start = ((), (), s32[]{:S(2)}) async-start(), calls=%async_computation.2 | async-start | bytes 3538944 | tf_op jit(solution)/shard_map/reduce_scatter | solution.py:47
  59.1 7.6 %copy-start.5 = (u32[128]{0:T(128)S(1)}, u32[128]{0:T(128)}, u32[]{:S(2)}) copy-start(u32[128]{0:T(128)} %constant.11) | copy-start | bytes 1540
  59.1 8.8 %copy-start.3 = (s32[4,8]{1,0:T(4,128)S(1)}, s32[4,8]{1,0:T(4,128)}, u32[]{:S(2)}) copy-start(s32[4,8]{1,0:T(4,128)} %param.13) | copy-start | bytes 388
  59.1 124.9 %copy-start.4 = (f32[4,8]{1,0:T(4,128)S(1)}, f32[4,8]{1,0:T(4,128)}, u32[]{:S(2)}) copy-start(f32[4,8]{1,0:T(4,128)} %param.15) | copy-start | bytes 388
Sparse Core Ops, SparseCore 0:
  66.8 33.1 reduce-scatter.1
